TPU v7x, 512 devices: a whole 4x4x16 slice. The times are simulated.
512 devices in a mesh: sub: 128 (over y, z, core), case: 4 (over x).
Axes of the slice: x: 4, y: 4, z: 16, core: 2. Of those that a mesh axis runs over, the one named last changes fastest.
Arguments:
- load_interior: float32 [128, 128, 4096], P('sub', None, 'case'), may hold values from -6 to 6
- load_boundary: float32 [128, 128, 1024], P('sub', None, 'case'), may hold values from -6 to 6
- cond_blocks: float32 [128, 128, 4096], P('sub', 'case'), may hold values from -0.25 to 0.25
- block_rows: int32 [128, 128], P('sub', 'case'), may hold values from 0 to 15
- block_cols: int32 [128, 128], P('sub', 'case'), may hold values from 0 to 63, as said below
- interface_maps: int32 [128, 7, 2, 1024], P('sub'), may hold values from 0 to 1023, as said below
- merge_maps: float32 [128, 7, 1024, 512], P('sub', None, 'case'), as said below
Outputs:
- leaf_loads: float32 [128, 1024, 128], P('sub', 'case')
- node_loads: float32 [128, 1024, 128], P('sub', 'case')
Inputs may be any that keep to these rules, and one draw needn't show every extreme that they name: `block_cols`: entry k of a substructure's row lies in [(k // 32) * 16, (k // 32 + 1) * 16); blocks may repeat. `interface_maps`: each row of 1024 entries is a permutation; at level index l, slots that agree in all but their lowest l + 1 bits hold equal entries. `merge_maps`: at level index l, slots that agree in all but their lowest l + 1 bits hold equal entries.
All inputs are finite; a program needn't handle non-finite values.
Results may differ from a plain program's by a relative error of at most 0.0003.
Values sent between devices are 32-bit elements; how exact they have to be, the bound alone decides.
No kernel may reach another device: no remote copies, remote signals or barrier semaphores. Data moves between devices by JAX's collectives and lax.ppermute only.
A program may use at most 64 MiB of HBM per device.

v0:
```python
import jax
import jax.numpy as jnp
from jax import lax
from jax.sharding import PartitionSpec as P

BLK = 64


def from_partner(value, axis, distance):
    mask = 2**distance
    pairs = [(source, source ^ mask) for source in range(lax.axis_size(axis))]
    return lax.ppermute(value, axis, pairs)


def to_row_quarters(value):
    return lax.all_to_all(value, "case", split_axis=0, concat_axis=1, tiled=True)


def on_device(
    load_interior, load_boundary, cond_blocks, block_rows, block_cols, interface_maps, merge_maps
):
    groups = lax.axis_size("case")
    local_rows = load_interior.shape[2]
    quarter = load_boundary.shape[2]
    full_rows = quarter * groups
    interior_rows = local_rows * groups
    block_size = BLK
    blocks = lax.all_gather(cond_blocks[0], "case", axis=0, tiled=True)
    rows_of_blocks = lax.all_gather(block_rows[0], "case", axis=0, tiled=True)
    cols_of_blocks = lax.all_gather(block_cols[0], "case", axis=0, tiled=True)
    block_count = blocks.shape[0]
    blocks = blocks.reshape(block_count, block_size, block_size)
    joined = jnp.concatenate([load_interior, load_boundary], axis=2)
    joined = lax.all_to_all(joined, "sub", split_axis=1, concat_axis=0, tiled=True)[:, 0, :]
    joined = lax.all_to_all(joined, "case", split_axis=0, concat_axis=1, tiled=True)
    num_cases = joined.shape[0]
    parts = joined.reshape(num_cases, groups, local_rows + quarter)
    interior = jnp.transpose(parts[:, :, :local_rows].reshape(num_cases, interior_rows))
    boundary = jnp.transpose(parts[:, :, local_rows:].reshape(num_cases, full_rows))
    pieces = jnp.take(
        interior.reshape(interior_rows // block_size, block_size, num_cases), cols_of_blocks, axis=0
    )
    products = jnp.einsum("krc,kcn->krn", blocks, pieces, precision=lax.Precision.HIGH)
    row_blocks = full_rows // block_size
    onehot = (rows_of_blocks[None, :] == jnp.arange(row_blocks, dtype=jnp.int32)[:, None]).astype(
        jnp.float32
    )
    summed = jnp.dot(
        onehot, products.reshape(block_count, block_size * num_cases), precision=lax.Precision.HIGH
    )
    leaf = boundary - summed.reshape(full_rows, num_cases)
    leaf_share = to_row_quarters(leaf)
    slot = lax.axis_index("sub")
    levels = lax.axis_size("sub").bit_length() - 1
    current = leaf
    nodes = jnp.zeros_like(leaf)
    for level in range(1, levels + 1):
        half = 1 << level - 1
        maps = interface_maps[0, level - 1]
        matrix = lax.all_gather(merge_maps[0, level - 1], "case", axis=0, tiled=True)
        shared_rows = matrix.shape[1]
        upper = slot // half % 2 == 1
        other = from_partner(current, "sub", level - 1)
        stacked = jnp.concatenate([current, other], axis=0)

        def left_index(index):
            return jnp.where(upper, index + full_rows, index)

        def right_index(index):
            return jnp.where(upper, index, index + full_rows)

        shared = jnp.take(stacked, left_index(maps[0, :shared_rows]), axis=0) + jnp.take(
            stacked, right_index(maps[1, :shared_rows]), axis=0
        )
        kept_index = jnp.concatenate(
            [left_index(maps[0, shared_rows:]), right_index(maps[1, shared_rows:])]
        )
        parent = jnp.take(stacked, kept_index, axis=0) - jnp.dot(
            matrix, shared, precision=lax.Precision.HIGH
        )
        is_node = slot % (2 * half) == half
        if level == levels:
            is_node = jnp.logical_or(is_node, slot == 0)
        nodes = jnp.where(is_node, parent, nodes)
        current = parent
    return (leaf_share[None], to_row_quarters(nodes)[None])


def solution(mesh):
    placed = (
        P("sub", None, "case"),
        P("sub", None, "case"),
        P("sub", "case", None),
        P("sub", "case"),
        P("sub", "case"),
        P("sub", None, None, None),
        P("sub", None, "case", None),
    )
    return jax.shard_map(
        on_device,
        mesh=mesh,
        in_specs=placed,
        out_specs=(P("sub", "case", None), P("sub", "case", None)),
        check_vma=False,
    )
```

profile of v0, /device:TPU:8, one launch (start us, length us, event | category | flops | bytes accessed | tf_op | source)
XLA Modules:
  0.0 363.9 jit_solution(5309197116855584580)
XLA Ops:
  7.2 2.4 copy.236
  9.6 3.9 %fusion.110 = (f32[1,1,256,512]{3,2,1,0:T(8,128)}, f32[1,1,256,512]{3,2,1,0:T(8,128)}, f32[1,1,256,512]{3,2,1,0:T(8,128)}, f32[1,1,256,512]{3,2,1,0:T(8,128)}, f...) fusion(f32[1,7,256,512]{3,2,1,0:T(8,128)} %param.17), kind=kLoop, calls=%fused_computation.216 | loop fusion | bytes 7340032 | tf_op jit(solution)/shard_map/slice | solution.py:60
  16.9 1.5 copy.232
  18.4 19.6 %all-to-all-start = ((f32[1,128,1280]{2,0,1:T(1,128)}), f32[1,128,1280]{2,0,1:T(1,128)S(1)}, u32[]{:S(2)}, u32[]{:S(2)}) async-start(f32[1,128,1280]{2,0,1:T(1,128)} %copy.232), calls=%async_computation | async-start | bytes 1310720 | tf_op jit(solution)/shard_map/all_to_all | solution.py:34
  38.8 1.3 dynamic-slice
  40.9 9.0 %all-reduce.2 = (s32[128]{0:T(128)S(1)}, s32[128]{0:T(128)S(1)}) all-reduce(s32[128]{0:T(128)S(1)} %bitcast_dynamic-update-slice_fusion, s32[128]{0:T(128)S(1)} %bitcast_dynamic-update-slice_fusion.1), channel_id=3, replica_groups=mesh['sub'=128,'case'=4] {'case'}, use_global_device_ids=true, to_apply=%add.1 | all-reduce | flops 256 | bytes 2048 | tf_op jit(solution)/shard_map/all_gather | solution.py:30
  50.8 26.4 %all-to-all-done = f32[1,128,1280]{2,0,1:T(1,128)S(1)} async-done(((f32[1,128,1280]{2,0,1:T(1,128)}), f32[1,128,1280]{2,0,1:T(1,128)S(1)}, u32[]{:S(2)}, u32[]{:S(2)}) %all-to-all-start) | async-done | bytes 655392 | tf_op jit(solution)/shard_map/all_to_all | solution.py:34
  78.2 4.3 %all-to-all-start.1 = ((f32[4,32,1280]{2,1,0:T(8,128)}), f32[4,32,1280]{2,1,0:T(8,128)S(1)}, u32[]{:S(2)}, u32[]{:S(2)}) async-start(f32[4,32,1280]{2,1,0:T(8,128)} %bitcast.67), calls=%async_computation.1 | async-start | bytes 1310720 | tf_op jit(solution)/shard_map/all_to_all | solution.py:35
  82.5 18.3 %all-to-all-done.1 = f32[4,32,1280]{2,1,0:T(8,128)S(1)} async-done(((f32[4,32,1280]{2,1,0:T(8,128)}), f32[4,32,1280]{2,1,0:T(8,128)S(1)}, u32[]{:S(2)}, u32[]{:S(2)}) %all-to-all-start.1) | async-done | bytes 655392 | tf_op jit(solution)/shard_map/all_to_all | solution.py:35
  103.9 5.6 %copy.237 = f32[1,128,4096]{1,2,0:T(8,128)} copy(f32[1,128,4096]{2,0,1:T(1,128)} %all-gather.19.cloned.1.call-done) | data formatting | bytes 4194304 | tf_op jit(solution)/shard_map/all_gather | solution.py:28
  109.5 5.6 %copy.238 = f32[128,64,64]{2,1,0:T(8,128)} copy(f32[128,64,64]{0,2,1:T(8,128)} %bitcast.158) | data formatting | bytes 4194304 | tf_op jit(solution)/shard_map/reshape | solution.py:32
  115.1 7.0 %fusion.16 = f32[128,64,32]{1,2,0:T(8,128)} fusion(f32[128,64,64]{2,1,0:T(8,128)} %copy.238, f32[128,64,32]{1,2,0:T(8,128)S(1)} %gather_fusion, pred[128]{0:T(512)(128)(4,1)S(1)} %compare_and_fusion.21), kind=kOutput, calls=%fused_computation.38 | convolution fusion | flops 100925440 | bytes 4194432 | tf_op jit(solution)/shard_map/krc,kcn->krn/dot_general | solution.py:43
  122.1 3.1 copy.239
  125.8 1.9 collective-permute-start
  127.8 1.8 collective-permute-done
  129.7 2.8 gather_fusion.1
  134.8 2.9 select_subtract_fusion
  137.8 3.2 collective-permute-start.1
  141.0 4.2 %collective-permute-done.1 = f32[1024,32]{0,1:T(8,128)S(1)} collective-permute-done((f32[1024,32]{0,1:T(8,128)S(1)}, f32[1024,32]{0,1:T(8,128)S(1)}, u32[]{:S(2)}, u32[]{:S(2)}) %collective-permute-start.1) | collective-permute-done | bytes 131104 | tf_op jit(solution)/shard_map/ppermute | solution.py:12
  145.5 2.8 gather_fusion.4
  150.6 2.9 fusion.25
  153.5 2.2 collective-permute-start.2
  155.8 8.0 %collective-permute-done.2 = f32[1024,32]{0,1:T(8,128)S(1)} collective-permute-done((f32[1024,32]{0,1:T(8,128)S(1)}, f32[1024,32]{0,1:T(8,128)S(1)}, u32[]{:S(2)}, u32[]{:S(2)}) %collective-permute-start.2) | collective-permute-done | bytes 131104 | tf_op jit(solution)/shard_map/ppermute | solution.py:12
  164.1 2.8 gather_fusion.7
  169.2 11.5 %all-gather.25.cloned.1.call-done = f32[1,1,1024,512]{3,2,1,0:T(8,128)} async-done(((f32[1,1,256,512]{3,2,1,0:T(8,128)}), f32[1,1,1024,512]{3,2,1,0:T(8,128)}) %all-gather.25.cloned.1.call-update) | async-done | bytes 2097168 | tf_op jit(solution)/shard_map/all_gather | solution.py:60
  180.7 2.9 fusion.31
  183.6 7.6 %collective-permute-start.3 = (f32[1024,32]{0,1:T(8,128)S(1)}, f32[1024,32]{0,1:T(8,128)S(1)}, u32[]{:S(2)}, u32[]{:S(2)}) collective-permute-start(f32[1024,32]{0,1:T(8,128)S(1)} %fusion.31), channel_id=1, source_target_pairs={{0,32},{4,36},{8,40},{12,44},{16,48},{20,52},{24,56},{28,60},{32,0... | collective-permute-start | bytes 393224 | tf_op jit(solution)/shard_map/ppermute | solution.py:12
  191.3 11.9 %collective-permute-done.3 = f32[1024,32]{0,1:T(8,128)S(1)} collective-permute-done((f32[1024,32]{0,1:T(8,128)S(1)}, f32[1024,32]{0,1:T(8,128)S(1)}, u32[]{:S(2)}, u32[]{:S(2)}) %collective-permute-start.3) | collective-permute-done | bytes 131104 | tf_op jit(solution)/shard_map/ppermute | solution.py:12
  203.5 2.8 gather_fusion.10
  208.6 12.7 %all-gather.27.cloned.1.call-done = f32[1,1,1024,512]{3,2,1,0:T(8,128)} async-done(((f32[1,1,256,512]{3,2,1,0:T(8,128)}), f32[1,1,1024,512]{3,2,1,0:T(8,128)}) %all-gather.27.cloned.1.call-update) | async-done | bytes 2097168 | tf_op jit(solution)/shard_map/all_gather | solution.py:60
  221.3 2.9 fusion.37
  224.2 12.8 %collective-permute-start.4 = (f32[1024,32]{0,1:T(8,128)S(1)}, f32[1024,32]{0,1:T(8,128)S(1)}, u32[]{:S(2)}, u32[]{:S(2)}) collective-permute-start(f32[1024,32]{0,1:T(8,128)S(1)} %fusion.37), channel_id=1, source_target_pairs={{0,64},{4,68},{8,72},{12,76},{16,80},{20,84},{24,88},{28,92},{32,9... | collective-permute-start | bytes 393224 | tf_op jit(solution)/shard_map/ppermute | solution.py:12
  237.0 3.7 %collective-permute-done.4 = f32[1024,32]{0,1:T(8,128)S(1)} collective-permute-done((f32[1024,32]{0,1:T(8,128)S(1)}, f32[1024,32]{0,1:T(8,128)S(1)}, u32[]{:S(2)}, u32[]{:S(2)}) %collective-permute-start.4) | collective-permute-done | bytes 131104 | tf_op jit(solution)/shard_map/ppermute | solution.py:12
  241.2 2.8 gather_fusion.13
  246.2 15.7 %all-gather.29.cloned.1.call-done = f32[1,1,1024,512]{3,2,1,0:T(8,128)} async-done(((f32[1,1,256,512]{3,2,1,0:T(8,128)}), f32[1,1,1024,512]{3,2,1,0:T(8,128)}) %all-gather.29.cloned.1.call-update) | async-done | bytes 2097168 | tf_op jit(solution)/shard_map/all_gather | solution.py:60
  261.9 2.9 fusion.43
  264.8 2.4 collective-permute-start.5
  267.3 4.6 %collective-permute-done.5 = f32[1024,32]{0,1:T(8,128)S(1)} collective-permute-done((f32[1024,32]{0,1:T(8,128)S(1)}, f32[1024,32]{0,1:T(8,128)S(1)}, u32[]{:S(2)}, u32[]{:S(2)}) %collective-permute-start.5) | collective-permute-done | bytes 131104 | tf_op jit(solution)/shard_map/ppermute | solution.py:12
  272.3 2.8 gather_fusion.16
  277.4 25.3 %all-gather.31.cloned.1.call-done = f32[1,1,1024,512]{3,2,1,0:T(8,128)} async-done(((f32[1,1,256,512]{3,2,1,0:T(8,128)}), f32[1,1,1024,512]{3,2,1,0:T(8,128)}) %all-gather.31.cloned.1.call-update) | async-done | bytes 2097168 | tf_op jit(solution)/shard_map/all_gather | solution.py:60
  302.7 2.9 fusion.49
  305.6 4.0 %collective-permute-start.6 = (f32[1024,32]{0,1:T(8,128)S(1)}, f32[1024,32]{0,1:T(8,128)S(1)}, u32[]{:S(2)}, u32[]{:S(2)}) collective-permute-start(f32[1024,32]{0,1:T(8,128)S(1)} %fusion.49), channel_id=1, source_target_pairs={{0,256},{4,260},{8,264},{12,268},{16,272},{20,276},{24,280},{28,28... | collective-permute-start | bytes 393224 | tf_op jit(solution)/shard_map/ppermute | solution.py:12
  310.5 3.3 all-to-all-start.2
  314.6 2.8 gather_fusion.19
  319.6 23.8 %all-gather.33.cloned.1.call-done = f32[1,1,1024,512]{3,2,1,0:T(8,128)} async-done(((f32[1,1,256,512]{3,2,1,0:T(8,128)}), f32[1,1,1024,512]{3,2,1,0:T(8,128)}) %all-gather.33.cloned.1.call-update) | async-done | bytes 2097168 | tf_op jit(solution)/shard_map/all_gather | solution.py:60
  343.5 2.9 fusion.58
  347.0 3.3 all-to-all-start.3
  351.1 5.2 %all-to-all-done.3 = f32[4,256,32]{1,2,0:T(8,128)S(1)} async-done(((f32[4,256,32]{1,2,0:T(8,128)}), f32[4,256,32]{1,2,0:T(8,128)S(1)}, u32[]{:S(2)}, u32[]{:S(2)}) %all-to-all-start.3) | async-done | bytes 131104 | tf_op jit(solution)/shard_map/all_to_all | solution.py:16
  (149 shorter events, 30.5 us)
Async XLA Ops:
  7.2 96.7 %all-gather.19.cloned.1.call-start = ((), (), s32[]{:S(2)}) async-start(), calls=%async_computation.4 | async-start | bytes 2621440 | tf_op jit(solution)/shard_map/all_gather | solution.py:28
  9.6 125.2 %all-gather.21.cloned.1.call-start = ((), (), s32[]{:S(2)}) async-start(), calls=%async_computation.5 | async-start | bytes 2621440 | tf_op jit(solution)/shard_map/all_gather | solution.py:60
  13.5 3.3 copy-start.1
  13.5 3.3 copy-start.2
  13.6 137.0 %all-gather.23.cloned.1.call-start = ((), (), s32[]{:S(2)}) async-start(), calls=%async_computation.6 | async-start | bytes 2621440 | tf_op jit(solution)/shard_map/all_gather | solution.py:60
  14.3 166.4 %all-gather.25.cloned.1.call-start = ((), (), s32[]{:S(2)}) async-start(), calls=%async_computation.7 | async-start | bytes 2621440 | tf_op jit(solution)/shard_map/all_gather | solution.py:60
  14.9 206.4 %all-gather.27.cloned.1.call-start = ((), (), s32[]{:S(2)}) async-start(), calls=%async_computation.8 | async-start | bytes 2621440 | tf_op jit(solution)/shard_map/all_gather | solution.py:60
  15.5 246.4 %all-gather.29.cloned.1.call-start = ((), (), s32[]{:S(2)}) async-start(), calls=%async_computation.9 | async-start | bytes 2621440 | tf_op jit(solution)/shard_map/all_gather | solution.py:60
  16.0 286.6 %all-gather.31.cloned.1.call-start = ((), (), s32[]{:S(2)}) async-start(), calls=%async_computation.10 | async-start | bytes 2621440 | tf_op jit(solution)/shard_map/all_gather | solution.py:60
  16.8 23.9 %copy-start.4 = (s32[1,32]{1,0:T(1,128)S(1)}, s32[1,32]{1,0:T(1,128)}, u32[]{:S(2)}) copy-start(s32[1,32]{1,0:T(1,128)} %param.15) | copy-start | bytes 388
  16.8 24.0 %copy-start.5 = (s32[1,32]{1,0:T(1,128)S(1)}, s32[1,32]{1,0:T(1,128)}, u32[]{:S(2)}) copy-start(s32[1,32]{1,0:T(1,128)} %param.14) | copy-start | bytes 388
  16.8 33.2 %copy-start.3 = (s32[1,7,2,1024]{3,2,1,0:T(2,128)S(1)}, s32[1,7,2,1024]{3,2,1,0:T(2,128)}, u32[]{:S(2)}) copy-start(s32[1,7,2,1024]{3,2,1,0:T(2,128)} %param.16) | copy-start | bytes 172036
  18.4 58.9 %all-to-all-start = ((f32[1,128,1280]{2,0,1:T(1,128)}), f32[1,128,1280]{2,0,1:T(1,128)S(1)}, u32[]{:S(2)}, u32[]{:S(2)}) async-start(f32[1,128,1280]{2,0,1:T(1,128)} %copy.232), calls=%async_computation | async-start | bytes 1310720 | tf_op jit(solution)/shard_map/all_to_all | solution.py:34
  38.0 305.4 %all-gather.33.cloned.1.call-start = ((), (), s32[]{:S(2)}) async-start(), calls=%async_computation.11 | async-start | bytes 2621440 | tf_op jit(solution)/shard_map/all_gather | solution.py:60
  78.2 22.6 %all-to-all-start.1 = ((f32[4,32,1280]{2,1,0:T(8,128)}), f32[4,32,1280]{2,1,0:T(8,128)S(1)}, u32[]{:S(2)}, u32[]{:S(2)}) async-start(f32[4,32,1280]{2,1,0:T(8,128)} %bitcast.67), calls=%async_computation.1 | async-start | bytes 1310720 | tf_op jit(solution)/shard_map/all_to_all | solution.py:35
  122.1 3.6 %copy-start = (f32[32,4,256]{0,2,1:T(8,128)S(1)}, f32[32,4,256]{0,2,1:T(8,128)}, u32[]{:S(2)}) copy-start(f32[32,4,256]{0,2,1:T(8,128)} %copy.233) | copy-start | bytes 393220
  125.8 3.8 %collective-permute-start = (f32[1024,32]{1,0:T(8,128)S(1)}, f32[1024,32]{1,0:T(8,128)S(1)}, u32[]{:S(2)}, u32[]{:S(2)}) collective-permute-start(f32[1024,32]{1,0:T(8,128)S(1)} %bitcast_subtract_fusion), channel_id=1, source_target_pairs={{0,4},{4,0},{8,12},{12,8},{16,20},{20,16},{24,28},{28,24},{32,36},... | collective-permute-start | bytes 393224 | tf_op jit(solution)/shard_map/ppermute | solution.py:12
  137.8 7.4 %collective-permute-start.1 = (f32[1024,32]{0,1:T(8,128)S(1)}, f32[1024,32]{0,1:T(8,128)S(1)}, u32[]{:S(2)}, u32[]{:S(2)}) collective-permute-start(f32[1024,32]{0,1:T(8,128)S(1)} %select_subtract_fusion), channel_id=1, source_target_pairs={{0,8},{4,12},{8,0},{12,4},{16,24},{20,28},{24,16},{28,20},{32,40},... | collective-permute-start | bytes 393224 | tf_op jit(solution)/shard_map/ppermute | solution.py:12
  153.5 10.3 %collective-permute-start.2 = (f32[1024,32]{0,1:T(8,128)S(1)}, f32[1024,32]{0,1:T(8,128)S(1)}, u32[]{:S(2)}, u32[]{:S(2)}) collective-permute-start(f32[1024,32]{0,1:T(8,128)S(1)} %fusion.25), channel_id=1, source_target_pairs={{0,16},{4,20},{8,24},{12,28},{16,0},{20,4},{24,8},{28,12},{32,48},... | collective-permute-start | bytes 393224 | tf_op jit(solution)/shard_map/ppermute | solution.py:12
  183.6 19.6 %collective-permute-start.3 = (f32[1024,32]{0,1:T(8,128)S(1)}, f32[1024,32]{0,1:T(8,128)S(1)}, u32[]{:S(2)}, u32[]{:S(2)}) collective-permute-start(f32[1024,32]{0,1:T(8,128)S(1)} %fusion.31), channel_id=1, source_target_pairs={{0,32},{4,36},{8,40},{12,44},{16,48},{20,52},{24,56},{28,60},{32,0... | collective-permute-start | bytes 393224 | tf_op jit(solution)/shard_map/ppermute | solution.py:12
  224.2 16.6 %collective-permute-start.4 = (f32[1024,32]{0,1:T(8,128)S(1)}, f32[1024,32]{0,1:T(8,128)S(1)}, u32[]{:S(2)}, u32[]{:S(2)}) collective-permute-start(f32[1024,32]{0,1:T(8,128)S(1)} %fusion.37), channel_id=1, source_target_pairs={{0,64},{4,68},{8,72},{12,76},{16,80},{20,84},{24,88},{28,92},{32,9... | collective-permute-start | bytes 393224 | tf_op jit(solution)/shard_map/ppermute | solution.py:12
  264.8 7.1 %collective-permute-start.5 = (f32[1024,32]{0,1:T(8,128)S(1)}, f32[1024,32]{0,1:T(8,128)S(1)}, u32[]{:S(2)}, u32[]{:S(2)}) collective-permute-start(f32[1024,32]{0,1:T(8,128)S(1)} %fusion.43), channel_id=1, source_target_pairs={{0,128},{4,132},{8,136},{12,140},{16,144},{20,148},{24,152},{28,15... | collective-permute-start | bytes 393224 | tf_op jit(solution)/shard_map/ppermute | solution.py:12
  305.6 8.6 %collective-permute-start.6 = (f32[1024,32]{0,1:T(8,128)S(1)}, f32[1024,32]{0,1:T(8,128)S(1)}, u32[]{:S(2)}, u32[]{:S(2)}) collective-permute-start(f32[1024,32]{0,1:T(8,128)S(1)} %fusion.49), channel_id=1, source_target_pairs={{0,256},{4,260},{8,264},{12,268},{16,272},{20,276},{24,280},{28,28... | collective-permute-start | bytes 393224 | tf_op jit(solution)/shard_map/ppermute | solution.py:12
  310.5 36.5 %all-to-all-start.2 = ((f32[4,256,32]{1,2,0:T(8,128)}), f32[4,256,32]{1,2,0:T(8,128)S(1)}, u32[]{:S(2)}, u32[]{:S(2)}) async-start(f32[4,256,32]{1,2,0:T(8,128)} %copy.240), calls=%async_computation.2 | async-start | bytes 262144 | tf_op jit(solution)/shard_map/all_to_all | solution.py:16
  347.0 9.3 %all-to-all-start.3 = ((f32[4,256,32]{1,2,0:T(8,128)}), f32[4,256,32]{1,2,0:T(8,128)S(1)}, u32[]{:S(2)}, u32[]{:S(2)}) async-start(f32[4,256,32]{1,2,0:T(8,128)} %bitcast.157), calls=%async_computation.3 | async-start | bytes 262144 | tf_op jit(solution)/shard_map/all_to_all | solution.py:16
Sparse Core Ops, SparseCore 0:
  10.1 42.9 all-gather.18
  55.2 45.4 all-gather.20
  102.8 37.2 all-gather.22
  142.1 38.5 all-gather.24
  182.7 38.5 all-gather.26
  223.2 38.5 all-gather.28
  264.0 38.6 all-gather.30
  304.8 38.6 all-gather.32
where the time goes:
time: 365 us; the launch traced here: 364 us
  waiting for transfers between devices  177 us (48%)
  local copies, waits for them, and re-layouts  68 us (19%)
  starting transfers between devices  65.1 us (18%)
  matrix products  27.6 us (8%)
  between operations  16.1 us (4%)
  blocking collectives  9.04 us (2%)
    all_gather x7, waiting for transfers between devices, on_device(): lax.all_gather(merge_maps[0, level - 1], 'case', axis=0, tiled=True)  89 us
    ppermute x7, waiting for transfers between devices, from_partner(): return lax.ppermute(value, axis, pairs)  34.6 us
    ppermute x7, starting transfers between devices, from_partner(): return lax.ppermute(value, axis, pairs)  34.3 us
    all_to_all x1, waiting for transfers between devices, on_device(): lax.all_to_all(joined, 'sub', split_axis=1, concat_axis=0, tiled=True)  26.4 us
    gather x14, local copies, waits for them, and re-layouts, on_device(): jnp.take(stacked, kept_index, axis=0)  20.9 us
    dot_general x7, matrix products, on_device(): jnp.dot(matrix, shared, precision=lax.Precision.HIGH)  20.2 us
    all_to_all x1, starting transfers between devices, on_device(): lax.all_to_all(joined, 'sub', split_axis=1, concat_axis=0, tiled=True)  19.6 us
    all_to_all x1, waiting for transfers between devices, on_device(): lax.all_to_all(joined, 'case', split_axis=0, concat_axis=1, tiled=True)  18.3 us
  transfers between devices with their start and end apart: 19, of which 15 were waited for; matrix products, arithmetic and copies ran while one was open for 26% of the time, Pallas kernels for 0%

commit v1 on v0

--- a/solution.py
+++ b/solution.py
@@ -57,7 +57,15 @@
     for level in range(1, levels + 1):
         half = 1 << level - 1
         maps = interface_maps[0, level - 1]
-        matrix = lax.all_gather(merge_maps[0, level - 1], "case", axis=0, tiled=True)
+        matrix = jnp.concatenate(
+            jax.lax.all_to_all(
+                jnp.stack(jax.lax.axis_size("case") * [merge_maps[0, level - 1]], axis=0),
+                "case",
+                0,
+                0,
+            ),
+            axis=0,
+        )
         shared_rows = matrix.shape[1]
         upper = slot // half % 2 == 1
         other = from_partner(current, "sub", level - 1)

time: 365 us -> 424 us (1.16)
  waiting for transfers between devices: 177 us -> 125 us
  local copies, waits for them, and re-layouts: 68 us -> 101 us
  blocking collectives: 9.04 us -> 37.8 us
  other arithmetic: 0.76 us -> 27.3 us
  starting transfers between devices: 65.1 us -> 88.8 us
    all_gather x7 -> x0, waiting for transfers between devices: 89 us -> none  [on_device(): lax.all_gather(merge_maps[0, level - 1], 'case', axis=0, tiled=True)]
    all_to_all x0 -> x7, waiting for transfers between devices: none -> 39.4 us  [on_device(): jax.lax.all_to_all(jnp.stack(jax.lax.axis_size('case') * [merge_maps[0, l...]
    all_to_all x0 -> x7, starting transfers between devices: none -> 30.6 us  [on_device(): jax.lax.all_to_all(jnp.stack(jax.lax.axis_size('case') * [merge_maps[0, l...]
    all_gather x1, blocking collectives: 9.04 us -> 37.8 us  [on_device(): cols_of_blocks = lax.all_gather(block_cols[0], 'case', axis=0, tiled=True)]
    another operation x0 -> x8, local copies, waits for them, and re-layouts: none -> 17.2 us  [on_device(): jnp.stack(jax.lax.axis_size('case') * [merge_maps[0, level - 1]], axis=0)]
    gather x14, local copies, waits for them, and re-layouts: 20.9 us -> 31.5 us  [on_device(): jnp.take(stacked, kept_index, axis=0)]
    all_to_all x1, waiting for transfers between devices: 18.3 us -> 8.22 us  [on_device(): lax.all_to_all(joined, 'case', split_axis=0, concat_axis=1, tiled=True)]
    gather x21, other arithmetic: 0.16 us -> 10.2 us
  transfers between devices with their start and end apart: 19 -> 19, of which waited for: 15 -> 11; matrix products, arithmetic and copies ran while one was open for 26% -> 36% of each run, Pallas kernels for 0% -> 0%
where the time goes in v1:
time: 424 us; the launch traced here: 422 us
  waiting for transfers between devices  125 us (29%)
  local copies, waits for them, and re-layouts  101 us (24%)
  starting transfers between devices  88.8 us (21%)
  blocking collectives  37.8 us (9%)
  other arithmetic  27.3 us (6%)
  matrix products  26.6 us (6%)
  between operations  15.6 us (4%)
    all_to_all x7, waiting for transfers between devices, on_device(): jax.lax.all_to_all(jnp.stack(jax.lax.axis_size('case') * [merge_maps[0, l...  39.4 us
    all_gather x1, blocking collectives, on_device(): cols_of_blocks = lax.all_gather(block_cols[0], 'case', axis=0, tiled=True)  37.8 us
    ppermute x7, waiting for transfers between devices, from_partner(): return lax.ppermute(value, axis, pairs)  34.7 us
    all_to_all x1, waiting for transfers between devices, on_device(): lax.all_to_all(joined, 'sub', split_axis=1, concat_axis=0, tiled=True)  34.6 us
    gather x14, local copies, waits for them, and re-layouts, on_device(): jnp.take(stacked, kept_index, axis=0)  31.5 us
    all_to_all x7, starting transfers between devices, on_device(): jax.lax.all_to_all(jnp.stack(jax.lax.axis_size('case') * [merge_maps[0, l...  30.6 us
    ppermute x7, starting transfers between devices, from_partner(): return lax.ppermute(value, axis, pairs)  24.3 us
    all_to_all x1, starting transfers between devices, on_device(): lax.all_to_all(joined, 'sub', split_axis=1, concat_axis=0, tiled=True)  22.6 us
  transfers between devices with their start and end apart: 19, of which 11 were waited for; matrix products, arithmetic and copies ran while one was open for 36% of the time, Pallas kernels for 0%

profile of v1, /device:TPU:8, one launch (start us, length us, event | category | flops | bytes accessed | tf_op | source)
XLA Modules:
  0.0 421.8 jit_solution(9002813800673230125)
XLA Ops:
  9.6 3.5 slice_bitcast_fusion.7
  14.8 4.4 %all-to-all-start.3 = ((f32[4,256,512]{2,1,0:T(8,128)}), f32[4,256,512]{2,1,0:T(8,128)S(1)}, u32[]{:S(2)}, u32[]{:S(2)}) async-start(f32[4,256,512]{2,1,0:T(8,128)} %stack.21), calls=%async_computation.3 | async-start | bytes 4194304 | tf_op jit(solution)/shard_map/all_to_all | solution.py:61
  21.4 37.8 %all-reduce.2 = (s32[128]{0:T(128)S(1)}, s32[128]{0:T(128)S(1)}) all-reduce(s32[128]{0:T(128)S(1)} %bitcast_dynamic-update-slice_fusion, s32[128]{0:T(128)S(1)} %bitcast_dynamic-update-slice_fusion.1), channel_id=3, replica_groups=mesh['sub'=128,'case'=4] {'case'}, use_global_device_ids=true, to_apply=%add.1 | all-reduce | flops 256 | bytes 2048 | tf_op jit(solution)/shard_map/all_gather | solution.py:30
  65.8 3.0 stack.22
  68.8 4.5 %all-to-all-start.4 = ((f32[4,256,512]{2,1,0:T(8,128)}), f32[4,256,512]{2,1,0:T(8,128)}, u32[]{:S(2)}, u32[]{:S(2)}) async-start(f32[4,256,512]{2,1,0:T(8,128)} %stack.22), calls=%async_computation.4 | async-start | bytes 4194304 | tf_op jit(solution)/shard_map/all_to_all | solution.py:61
  77.3 17.9 %all-to-all-done.4 = f32[4,256,512]{2,1,0:T(8,128)} async-done(((f32[4,256,512]{2,1,0:T(8,128)}), f32[4,256,512]{2,1,0:T(8,128)}, u32[]{:S(2)}, u32[]{:S(2)}) %all-to-all-start.4) | async-done | bytes 2097184 | tf_op jit(solution)/shard_map/all_to_all | solution.py:61
  95.3 22.6 %all-to-all-start = ((f32[1,128,1280]{2,0,1:T(1,128)}), f32[1,128,1280]{2,0,1:T(1,128)S(1)}, u32[]{:S(2)}, u32[]{:S(2)}) async-start(f32[1,128,1280]{2,0,1:T(1,128)} %copy.232), calls=%async_computation | async-start | bytes 1310720 | tf_op jit(solution)/shard_map/all_to_all | solution.py:34
  122.6 34.6 %all-to-all-done = f32[1,128,1280]{2,0,1:T(1,128)S(1)} async-done(((f32[1,128,1280]{2,0,1:T(1,128)}), f32[1,128,1280]{2,0,1:T(1,128)S(1)}, u32[]{:S(2)}, u32[]{:S(2)}) %all-to-all-start) | async-done | bytes 655392 | tf_op jit(solution)/shard_map/all_to_all | solution.py:34
  157.2 2.7 stack.23
  159.8 3.6 all-to-all-start.5
  167.7 21.5 %all-to-all-done.5 = f32[4,256,512]{2,1,0:T(8,128)S(1)} async-done(((f32[4,256,512]{2,1,0:T(8,128)}), f32[4,256,512]{2,1,0:T(8,128)S(1)}, u32[]{:S(2)}, u32[]{:S(2)}) %all-to-all-start.5) | async-done | bytes 2097184 | tf_op jit(solution)/shard_map/all_to_all | solution.py:61
  189.2 3.5 all-to-all-start.1
  193.9 8.2 %all-to-all-done.1 = f32[4,32,1280]{2,1,0:T(8,128)S(1)} async-done(((f32[4,32,1280]{2,1,0:T(8,128)}), f32[4,32,1280]{2,1,0:T(8,128)S(1)}, u32[]{:S(2)}, u32[]{:S(2)}) %all-to-all-start.1) | async-done | bytes 655392 | tf_op jit(solution)/shard_map/all_to_all | solution.py:35
  203.7 4.6 %all-to-all-start.6 = ((f32[4,256,512]{2,1,0:T(8,128)}), f32[4,256,512]{2,1,0:T(8,128)}, u32[]{:S(2)}, u32[]{:S(2)}) async-start(f32[4,256,512]{2,1,0:T(8,128)} %stack.24), calls=%async_computation.6 | async-start | bytes 4194304 | tf_op jit(solution)/shard_map/all_to_all | solution.py:61
  212.5 5.6 %copy.237 = f32[1,128,4096]{1,2,0:T(8,128)} copy(f32[1,128,4096]{2,0,1:T(1,128)} %all-gather.5.cloned.1.call-done) | data formatting | bytes 4194304 | tf_op jit(solution)/shard_map/all_gather | solution.py:28
  218.1 5.6 %copy.238 = f32[128,64,64]{2,1,0:T(8,128)} copy(f32[128,64,64]{0,2,1:T(8,128)} %bitcast.135) | data formatting | bytes 4194304 | tf_op jit(solution)/shard_map/reshape | solution.py:32
  223.8 6.9 %fusion.2 = f32[128,64,32]{1,2,0:T(8,128)} fusion(f32[128,64,64]{2,1,0:T(8,128)} %copy.238, f32[128,64,32]{1,2,0:T(8,128)S(1)} %gather_fusion, pred[128]{0:T(512)(128)(4,1)S(1)} %compare_and_fusion.21), kind=kOutput, calls=%fused_computation.24 | convolution fusion | flops 100925440 | bytes 4194432 | tf_op jit(solution)/shard_map/krc,kcn->krn/dot_general | solution.py:43
  230.7 3.1 copy.239
  238.0 4.6 %all-to-all-start.7 = ((f32[4,256,512]{2,1,0:T(8,128)}), f32[4,256,512]{2,1,0:T(8,128)}, u32[]{:S(2)}, u32[]{:S(2)}) async-start(f32[4,256,512]{2,1,0:T(8,128)} %stack.25), calls=%async_computation.7 | async-start | bytes 4194304 | tf_op jit(solution)/shard_map/all_to_all | solution.py:61
  243.9 2.8 gather_fusion.1
  252.6 3.0 collective-permute-start.1
  255.7 4.6 %collective-permute-done.1 = f32[1024,32]{0,1:T(8,128)S(1)} collective-permute-done((f32[1024,32]{0,1:T(8,128)S(1)}, f32[1024,32]{0,1:T(8,128)S(1)}, u32[]{:S(2)}, u32[]{:S(2)}) %collective-permute-start.1) | collective-permute-done | bytes 131104 | tf_op jit(solution)/shard_map/ppermute | solution.py:12
  260.6 2.8 gather_fusion.4
  265.8 2.9 fusion.11
  268.7 3.3 collective-permute-start.2
  274.2 4.6 %all-to-all-start.8 = ((f32[4,256,512]{2,1,0:T(8,128)}), f32[4,256,512]{2,1,0:T(8,128)}, u32[]{:S(2)}, u32[]{:S(2)}) async-start(f32[4,256,512]{2,1,0:T(8,128)} %stack.26), calls=%async_computation.8 | async-start | bytes 4194304 | tf_op jit(solution)/shard_map/all_to_all | solution.py:61
  279.7 2.8 gather_fusion.7
  289.1 3.4 collective-permute-start.3
  293.1 14.9 %collective-permute-done.3 = f32[1024,32]{0,1:T(8,128)S(1)} collective-permute-done((f32[1024,32]{0,1:T(8,128)S(1)}, f32[1024,32]{0,1:T(8,128)S(1)}, u32[]{:S(2)}, u32[]{:S(2)}) %collective-permute-start.3) | collective-permute-done | bytes 131104 | tf_op jit(solution)/shard_map/ppermute | solution.py:12
  308.3 2.8 gather_fusion.10
  313.5 2.9 fusion.9
  316.4 6.2 %collective-permute-start.4 = (f32[1024,32]{0,1:T(8,128)S(1)}, f32[1024,32]{0,1:T(8,128)S(1)}, u32[]{:S(2)}, u32[]{:S(2)}) collective-permute-start(f32[1024,32]{0,1:T(8,128)S(1)} %fusion.9), channel_id=1, source_target_pairs={{0,64},{4,68},{8,72},{12,76},{16,80},{20,84},{24,88},{28,92},{32,9... | collective-permute-start | bytes 393224 | tf_op jit(solution)/shard_map/ppermute | solution.py:12
  325.3 4.3 %all-to-all-start.9 = ((f32[4,256,512]{2,1,0:T(8,128)}), f32[4,256,512]{2,1,0:T(8,128)S(1)}, u32[]{:S(2)}, u32[]{:S(2)}) async-start(f32[4,256,512]{2,1,0:T(8,128)} %stack.27), calls=%async_computation.9 | async-start | bytes 4194304 | tf_op jit(solution)/shard_map/all_to_all | solution.py:61
  329.7 8.2 %collective-permute-done.4 = f32[1024,32]{0,1:T(8,128)S(1)} collective-permute-done((f32[1024,32]{0,1:T(8,128)S(1)}, f32[1024,32]{0,1:T(8,128)S(1)}, u32[]{:S(2)}, u32[]{:S(2)}) %collective-permute-start.4) | collective-permute-done | bytes 131104 | tf_op jit(solution)/shard_map/ppermute | solution.py:12
  339.9 4.3 %gather_fusion.13 = f32[1024,32]{1,0:T(8,128)} fusion(f32[2048,32]{1,0:T(8,128)S(1)} %copy.254, s32[1024]{0:T(1024)} %fusion.48), kind=kCustom, calls=%fused_computation.5.clone | custom fusion | bytes 266240 | tf_op jit(solution)/shard_map/jit(_take)/gather | solution.py:86
  349.7 3.1 fusion.8
  352.8 3.1 collective-permute-start.5
  356.5 3.6 collective-permute-done.5
  362.2 4.3 %gather_fusion.16 = f32[1024,32]{1,0:T(8,128)} fusion(f32[2048,32]{1,0:T(8,128)S(1)} %copy.258, s32[1024]{0:T(1024)} %fusion.49), kind=kCustom, calls=%fused_computation.6.clone | custom fusion | bytes 266240 | tf_op jit(solution)/shard_map/jit(_take)/gather | solution.py:86
  371.8 3.2 fusion.7
  375.0 3.5 collective-permute-start.6
  379.9 3.4 collective-permute-done.6
  385.4 4.0 gather_fusion.19
  394.5 4.5 %all-to-all-start.2 = ((f32[4,256,32]{1,2,0:T(8,128)}), f32[4,256,32]{1,2,0:T(8,128)S(1)}, u32[]{:S(2)}, u32[]{:S(2)}) async-start(f32[4,256,32]{1,2,0:T(8,128)} %copy.240), calls=%async_computation.2 | async-start | bytes 262144 | tf_op jit(solution)/shard_map/all_to_all | solution.py:16
  399.0 2.4 fusion.6
  402.1 2.9 all-to-all-done.2
  404.9 3.3 all-to-all-start.10
  409.0 5.2 %all-to-all-done.10 = f32[4,256,32]{1,2,0:T(8,128)S(1)} async-done(((f32[4,256,32]{1,2,0:T(8,128)}), f32[4,256,32]{1,2,0:T(8,128)S(1)}, u32[]{:S(2)}, u32[]{:S(2)}) %all-to-all-start.10) | async-done | bytes 131104 | tf_op jit(solution)/shard_map/all_to_all | solution.py:16
  (231 shorter events, 87.7 us)
Async XLA Ops:
  7.2 205.3 %all-gather.5.cloned.1.call-start = ((), (), s32[]{:S(2)}) async-start(), calls=%async_computation.11 | async-start | bytes 2621440 | tf_op jit(solution)/shard_map/all_gather | solution.py:28
  14.8 6.4 %copy-start.45 = (s32[1,32]{1,0:T(1,128)S(1)}, s32[1,32]{1,0:T(1,128)}, u32[]{:S(2)}) copy-start(s32[1,32]{1,0:T(1,128)} %param.15) | copy-start | bytes 388
  14.8 6.5 %copy-start.46 = (s32[1,32]{1,0:T(1,128)S(1)}, s32[1,32]{1,0:T(1,128)}, u32[]{:S(2)}) copy-start(s32[1,32]{1,0:T(1,128)} %param.14) | copy-start | bytes 388
  14.8 44.4 %copy-start.13 = (f32[1,128,256]{2,1,0:T(8,128)S(1)}, f32[1,128,256]{2,1,0:T(8,128)}, u32[]{:S(2)}) copy-start(f32[1,128,256]{2,1,0:T(8,128)} %param.12) | copy-start | bytes 393220
  14.8 51.0 %all-to-all-start.3 = ((f32[4,256,512]{2,1,0:T(8,128)}), f32[4,256,512]{2,1,0:T(8,128)S(1)}, u32[]{:S(2)}, u32[]{:S(2)}) async-start(f32[4,256,512]{2,1,0:T(8,128)} %stack.21), calls=%async_computation.3 | async-start | bytes 4194304 | tf_op jit(solution)/shard_map/all_to_all | solution.py:61
  68.8 26.5 %all-to-all-start.4 = ((f32[4,256,512]{2,1,0:T(8,128)}), f32[4,256,512]{2,1,0:T(8,128)}, u32[]{:S(2)}, u32[]{:S(2)}) async-start(f32[4,256,512]{2,1,0:T(8,128)} %stack.22), calls=%async_computation.4 | async-start | bytes 4194304 | tf_op jit(solution)/shard_map/all_to_all | solution.py:61
  95.3 61.9 %all-to-all-start = ((f32[1,128,1280]{2,0,1:T(1,128)}), f32[1,128,1280]{2,0,1:T(1,128)S(1)}, u32[]{:S(2)}, u32[]{:S(2)}) async-start(f32[1,128,1280]{2,0,1:T(1,128)} %copy.232), calls=%async_computation | async-start | bytes 1310720 | tf_op jit(solution)/shard_map/all_to_all | solution.py:34
  120.8 122.3 %copy-start.21 = (s32[512]{0:T(512)}, s32[512]{0:T(512)S(1)}, u32[]{:S(2)}) copy-start(s32[512]{0:T(512)S(1)} %add_select_fusion.22) | copy-start | bytes 6148
  120.9 122.3 %copy-start.23 = (s32[512]{0:T(512)}, s32[512]{0:T(512)S(1)}, u32[]{:S(2)}) copy-start(s32[512]{0:T(512)S(1)} %add_select_fusion.23) | copy-start | bytes 6148
  159.8 29.4 %all-to-all-start.5 = ((f32[4,256,512]{2,1,0:T(8,128)}), f32[4,256,512]{2,1,0:T(8,128)S(1)}, u32[]{:S(2)}, u32[]{:S(2)}) async-start(f32[4,256,512]{2,1,0:T(8,128)} %stack.23), calls=%async_computation.5 | async-start | bytes 4194304 | tf_op jit(solution)/shard_map/all_to_all | solution.py:61
  189.2 14.5 %copy-start.2 = (f32[4,256,512]{2,1,0:T(8,128)}, f32[4,256,512]{2,1,0:T(8,128)S(1)}, u32[]{:S(2)}) copy-start(f32[4,256,512]{2,1,0:T(8,128)S(1)} %all-to-all-done.5) | copy-start | bytes 6291460
  189.2 12.9 %all-to-all-start.1 = ((f32[4,32,1280]{2,1,0:T(8,128)}), f32[4,32,1280]{2,1,0:T(8,128)S(1)}, u32[]{:S(2)}, u32[]{:S(2)}) async-start(f32[4,32,1280]{2,1,0:T(8,128)} %bitcast.74), calls=%async_computation.1 | async-start | bytes 1310720 | tf_op jit(solution)/shard_map/all_to_all | solution.py:35
  203.7 32.7 %all-to-all-start.6 = ((f32[4,256,512]{2,1,0:T(8,128)}), f32[4,256,512]{2,1,0:T(8,128)}, u32[]{:S(2)}, u32[]{:S(2)}) async-start(f32[4,256,512]{2,1,0:T(8,128)} %stack.24), calls=%async_computation.6 | async-start | bytes 4194304 | tf_op jit(solution)/shard_map/all_to_all | solution.py:61
  234.4 9.3 %copy-start.4 = (f32[1024,32]{1,0:T(8,128)}, f32[1024,32]{1,0:T(8,128)S(1)}, u32[]{:S(2)}) copy-start(f32[1024,32]{1,0:T(8,128)S(1)} %bitcast_subtract_fusion) | copy-start | bytes 393220
  234.4 9.3 %collective-permute-start = (f32[1024,32]{1,0:T(8,128)S(1)}, f32[1024,32]{1,0:T(8,128)S(1)}, u32[]{:S(2)}, u32[]{:S(2)}) collective-permute-start(f32[1024,32]{1,0:T(8,128)S(1)} %bitcast_subtract_fusion), channel_id=1, source_target_pairs={{0,4},{4,0},{8,12},{12,8},{16,20},{20,16},{24,28},{28,24},{32,36},... | collective-permute-start | bytes 393224 | tf_op jit(solution)/shard_map/ppermute | solution.py:12
  238.0 34.6 %all-to-all-start.7 = ((f32[4,256,512]{2,1,0:T(8,128)}), f32[4,256,512]{2,1,0:T(8,128)}, u32[]{:S(2)}, u32[]{:S(2)}) async-start(f32[4,256,512]{2,1,0:T(8,128)} %stack.25), calls=%async_computation.7 | async-start | bytes 4194304 | tf_op jit(solution)/shard_map/all_to_all | solution.py:61
  250.2 5.4 %copy-start.22 = (s32[512]{0:T(512)S(1)}, s32[512]{0:T(512)}, u32[]{:S(2)}) copy-start(s32[512]{0:T(512)} %copy-done.21) | copy-start | bytes 6148
  250.2 5.4 %copy-start.24 = (s32[512]{0:T(512)S(1)}, s32[512]{0:T(512)}, u32[]{:S(2)}) copy-start(s32[512]{0:T(512)} %copy-done.23) | copy-start | bytes 6148
  250.2 5.4 %copy-start.17 = (s32[512]{0:T(512)S(1)}, s32[512]{0:T(512)}, u32[]{:S(2)}) copy-start(s32[512]{0:T(512)} %add_select_fusion.18) | copy-start | bytes 6148
  250.2 5.4 %copy-start.18 = (s32[512]{0:T(512)S(1)}, s32[512]{0:T(512)}, u32[]{:S(2)}) copy-start(s32[512]{0:T(512)} %add_select_fusion.19) | copy-start | bytes 6148
  250.2 10.4 %copy-start.26 = (s32[1024]{0:T(1024)S(1)}, s32[1024]{0:T(1024)}, u32[]{:S(2)}) copy-start(s32[1024]{0:T(1024)} %fusion.45) | copy-start | bytes 12292
  252.6 7.7 %collective-permute-start.1 = (f32[1024,32]{0,1:T(8,128)S(1)}, f32[1024,32]{0,1:T(8,128)S(1)}, u32[]{:S(2)}, u32[]{:S(2)}) collective-permute-start(f32[1024,32]{0,1:T(8,128)S(1)} %select_subtract_fusion), channel_id=1, source_target_pairs={{0,8},{4,12},{8,0},{12,4},{16,24},{20,28},{24,16},{28,20},{32,40},... | collective-permute-start | bytes 393224 | tf_op jit(solution)/shard_map/ppermute | solution.py:12
  264.7 7.9 %copy-start.7 = (f32[256,512]{1,0:T(8,128)S(1)}, f32[256,512]{1,0:T(8,128)}, u32[]{:S(2)}) copy-start(f32[256,512]{1,0:T(8,128)} %get-tuple-element.52) | copy-start | bytes 1572868
  268.7 10.7 %collective-permute-start.2 = (f32[1024,32]{0,1:T(8,128)S(1)}, f32[1024,32]{0,1:T(8,128)S(1)}, u32[]{:S(2)}, u32[]{:S(2)}) collective-permute-start(f32[1024,32]{0,1:T(8,128)S(1)} %fusion.11), channel_id=1, source_target_pairs={{0,16},{4,20},{8,24},{12,28},{16,0},{20,4},{24,8},{28,12},{32,48},... | collective-permute-start | bytes 393224 | tf_op jit(solution)/shard_map/ppermute | solution.py:12
  274.2 49.5 %all-to-all-start.8 = ((f32[4,256,512]{2,1,0:T(8,128)}), f32[4,256,512]{2,1,0:T(8,128)}, u32[]{:S(2)}, u32[]{:S(2)}) async-start(f32[4,256,512]{2,1,0:T(8,128)} %stack.26), calls=%async_computation.8 | async-start | bytes 4194304 | tf_op jit(solution)/shard_map/all_to_all | solution.py:61
  286.7 5.8 %copy-start.19 = (s32[512]{0:T(512)S(1)}, s32[512]{0:T(512)}, u32[]{:S(2)}) copy-start(s32[512]{0:T(512)} %add_select_fusion.10) | copy-start | bytes 6148
  286.7 5.8 %copy-start.20 = (s32[512]{0:T(512)S(1)}, s32[512]{0:T(512)}, u32[]{:S(2)}) copy-start(s32[512]{0:T(512)} %add_select_fusion.11) | copy-start | bytes 6148
  286.7 21.6 %copy-start.25 = (s32[1024]{0:T(1024)S(1)}, s32[1024]{0:T(1024)}, u32[]{:S(2)}) copy-start(s32[1024]{0:T(1024)} %fusion.47) | copy-start | bytes 12292
  289.1 18.9 %collective-permute-start.3 = (f32[1024,32]{0,1:T(8,128)S(1)}, f32[1024,32]{0,1:T(8,128)S(1)}, u32[]{:S(2)}, u32[]{:S(2)}) collective-permute-start(f32[1024,32]{0,1:T(8,128)S(1)} %fusion.10), channel_id=1, source_target_pairs={{0,32},{4,36},{8,40},{12,44},{16,48},{20,52},{24,56},{28,60},{32,0... | collective-permute-start | bytes 393224 | tf_op jit(solution)/shard_map/ppermute | solution.py:12
  312.4 10.7 %copy-start.15 = (s32[512]{0:T(512)S(1)}, s32[512]{0:T(512)}, u32[]{:S(2)}) copy-start(s32[512]{0:T(512)} %add_select_fusion.6) | copy-start | bytes 6148
  312.4 10.7 %copy-start.16 = (s32[512]{0:T(512)S(1)}, s32[512]{0:T(512)}, u32[]{:S(2)}) copy-start(s32[512]{0:T(512)} %add_select_fusion.7) | copy-start | bytes 6148
  312.4 11.3 %copy-start.6 = (f32[256,512]{1,0:T(8,128)S(1)}, f32[256,512]{1,0:T(8,128)}, u32[]{:S(2)}) copy-start(f32[256,512]{1,0:T(8,128)} %get-tuple-element.51) | copy-start | bytes 1572868
  316.4 21.5 %copy-start.10 = (f32[1024,32]{0,1:T(8,128)}, f32[1024,32]{0,1:T(8,128)S(1)}, u32[]{:S(2)}) copy-start(f32[1024,32]{0,1:T(8,128)S(1)} %fusion.9) | copy-start | bytes 393220
  316.4 21.4 %collective-permute-start.4 = (f32[1024,32]{0,1:T(8,128)S(1)}, f32[1024,32]{0,1:T(8,128)S(1)}, u32[]{:S(2)}, u32[]{:S(2)}) collective-permute-start(f32[1024,32]{0,1:T(8,128)S(1)} %fusion.9), channel_id=1, source_target_pairs={{0,64},{4,68},{8,72},{12,76},{16,80},{20,84},{24,88},{28,92},{32,9... | collective-permute-start | bytes 393224 | tf_op jit(solution)/shard_map/ppermute | solution.py:12
  325.3 69.2 %all-to-all-start.9 = ((f32[4,256,512]{2,1,0:T(8,128)}), f32[4,256,512]{2,1,0:T(8,128)S(1)}, u32[]{:S(2)}, u32[]{:S(2)}) async-start(f32[4,256,512]{2,1,0:T(8,128)} %stack.27), calls=%async_computation.9 | async-start | bytes 4194304 | tf_op jit(solution)/shard_map/all_to_all | solution.py:61
  352.8 7.3 %copy-start.11 = (f32[1024,32]{0,1:T(8,128)}, f32[1024,32]{0,1:T(8,128)S(1)}, u32[]{:S(2)}) copy-start(f32[1024,32]{0,1:T(8,128)S(1)} %fusion.8) | copy-start | bytes 393220
  352.8 7.3 %collective-permute-start.5 = (f32[1024,32]{0,1:T(8,128)S(1)}, f32[1024,32]{0,1:T(8,128)S(1)}, u32[]{:S(2)}, u32[]{:S(2)}) collective-permute-start(f32[1024,32]{0,1:T(8,128)S(1)} %fusion.8), channel_id=1, source_target_pairs={{0,128},{4,132},{8,136},{12,140},{16,144},{20,148},{24,152},{28,15... | collective-permute-start | bytes 393224 | tf_op jit(solution)/shard_map/ppermute | solution.py:12
  362.2 6.2 %copy-start.35 = (s32[1024]{0:T(1024)S(1)}, s32[1024]{0:T(1024)}, u32[]{:S(2)}) copy-start(s32[1024]{0:T(1024)} %pad_clamp_fusion.3) | copy-start | bytes 12292
  370.0 9.1 %copy-start.37 = (s32[512]{0:T(512)S(1)}, s32[512]{0:T(512)}, u32[]{:S(2)}) copy-start(s32[512]{0:T(512)} %get-tuple-element.21) | copy-start | bytes 6148
  371.8 7.3 %copy-start.5 = (f32[1024,32]{1,0:T(8,128)S(1)}, f32[1024,32]{1,0:T(8,128)}, u32[]{:S(2)}) copy-start(f32[1024,32]{1,0:T(8,128)} %copy-done.4) | copy-start | bytes 393220
  375.0 8.4 %copy-start.12 = (f32[1024,32]{0,1:T(8,128)}, f32[1024,32]{0,1:T(8,128)S(1)}, u32[]{:S(2)}) copy-start(f32[1024,32]{0,1:T(8,128)S(1)} %fusion.7) | copy-start | bytes 393220
  375.0 8.4 %collective-permute-start.6 = (f32[1024,32]{0,1:T(8,128)S(1)}, f32[1024,32]{0,1:T(8,128)S(1)}, u32[]{:S(2)}, u32[]{:S(2)}) collective-permute-start(f32[1024,32]{0,1:T(8,128)S(1)} %fusion.7), channel_id=1, source_target_pairs={{0,256},{4,260},{8,264},{12,268},{16,272},{20,276},{24,280},{28,28... | collective-permute-start | bytes 393224 | tf_op jit(solution)/shard_map/ppermute | solution.py:12
  385.4 5.9 %copy-start.33 = (s32[1024]{0:T(1024)S(1)}, s32[1024]{0:T(1024)}, u32[]{:S(2)}) copy-start(s32[1024]{0:T(1024)} %pad_clamp_fusion.1) | copy-start | bytes 12292
  391.2 7.7 %copy-start.38 = (pred[1024]{0:T(1024)(128)(4,1)S(1)}, pred[1024]{0:T(1024)(128)(4,1)}, u32[]{:S(2)}) copy-start(pred[1024]{0:T(1024)(128)(4,1)} %compare_and_fusion) | copy-start | bytes 3076
  391.2 7.7 %copy-start.41 = (pred[512]{0:T(512)(128)(4,1)S(1)}, pred[512]{0:T(512)(128)(4,1)}, u32[]{:S(2)}) copy-start(pred[512]{0:T(512)(128)(4,1)} %get-tuple-element.18) | copy-start | bytes 1540
  392.9 6.1 %copy-start.44 = (pred[512]{0:T(512)(128)(4,1)S(1)}, pred[512]{0:T(512)(128)(4,1)}, u32[]{:S(2)}) copy-start(pred[512]{0:T(512)(128)(4,1)} %get-tuple-element.20) | copy-start | bytes 1540
  394.5 10.4 %all-to-all-start.2 = ((f32[4,256,32]{1,2,0:T(8,128)}), f32[4,256,32]{1,2,0:T(8,128)S(1)}, u32[]{:S(2)}, u32[]{:S(2)}) async-start(f32[4,256,32]{1,2,0:T(8,128)} %copy.240), calls=%async_computation.2 | async-start | bytes 262144 | tf_op jit(solution)/shard_map/all_to_all | solution.py:16
  404.9 9.3 %all-to-all-start.10 = ((f32[4,256,32]{1,2,0:T(8,128)}), f32[4,256,32]{1,2,0:T(8,128)S(1)}, u32[]{:S(2)}, u32[]{:S(2)}) async-start(f32[4,256,32]{1,2,0:T(8,128)} %bitcast.134), calls=%async_computation.10 | async-start | bytes 262144 | tf_op jit(solution)/shard_map/all_to_all | solution.py:16
  (18 other events, 48.5 us)
Sparse Core Ops, SparseCore 0:
  10.1 52.7 all-gather.4
